TPU v7x, 512 devices: a whole 4x4x16 slice. The times are simulated.
512 devices in a mesh: band: 32 (over x, z_lo), grid: 16 (over z_hi, y, core).
Axes of the slice: x: 4, y: 4, z: 16 (z_hi: 2, z_lo: 8; z = z_hi * 8 + z_lo), core: 2. Of those that a mesh axis runs over, the one named last changes fastest.
Arguments:
- trial_bands: float32 [64, 160, 32, 128], P('band', 'grid'), may hold values from -6 to 6
- potential: float32 [160, 32, 128], P('grid'), may hold values from -2 to 0
Outputs:
- filtered: float32 [64, 160, 32, 128], P('band', 'grid')
- projected: float32 [64, 64], P('band')
- residual_norms: float32 [64], P('band')
All inputs are finite; a program needn't handle non-finite values.
Results may differ from a plain program's by a relative error of at most 0.00016.
Values sent between devices are 32-bit elements; how exact they have to be, the bound alone decides.
No kernel may reach another device: no remote copies, remote signals or barrier semaphores. Data moves between devices by JAX's collectives and lax.ppermute only.
A program may use at most 64 MiB of HBM per device.

v0:
```python
import jax
import jax.numpy as jnp
from jax import lax
from jax.sharding import PartitionSpec as P

CENTER = 4.25
HALF_WIDTH = 3.75
LOWEST = -2.0
SIGMA_ONE = HALF_WIDTH / (LOWEST - CENTER)
FOUR_THIRDS = 4.0 / 3.0
TWELFTH = 1.0 / 12.0
filter_degree = 4


def padded_2(cells, sides, width):
    for axis, dim in sides:
        count = lax.axis_size(axis)
        head = lax.slice_in_dim(cells, 0, width, axis=dim)
        tail = lax.slice_in_dim(cells, cells.shape[dim] - width, cells.shape[dim], axis=dim)
        cells = jnp.concatenate(
            [
                lax.ppermute(tail, axis, [(i, (i + 1) % count) for i in range(count)]),
                cells,
                lax.ppermute(head, axis, [((i + 1) % count, i) for i in range(count)]),
            ],
            axis=dim,
        )
    return cells


def operate(field_in, potential):
    padded = padded_2(field_in, (("grid", 1),), 2)
    plane_count = field_in.shape[1]
    near_sum = padded[:, 1 : 1 + plane_count] + padded[:, 3 : 3 + plane_count]
    near_sum = near_sum + jnp.roll(field_in, 1, 2) + jnp.roll(field_in, -1, 2)
    near_sum = near_sum + jnp.roll(field_in, 1, 3) + jnp.roll(field_in, -1, 3)
    far_sum = padded[:, 0:plane_count] + padded[:, 4 : 4 + plane_count]
    far_sum = far_sum + jnp.roll(field_in, 2, 2) + jnp.roll(field_in, -2, 2)
    far_sum = far_sum + jnp.roll(field_in, 2, 3) + jnp.roll(field_in, -2, 3)
    kinetic = 0.5 * (7.5 * field_in - FOUR_THIRDS * near_sum + TWELFTH * far_sum)
    return kinetic + potential * field_in


def on_device(trial_bands, potential):
    sigma_now = SIGMA_ONE
    previous = trial_bands
    current = (operate(trial_bands, potential) - CENTER * trial_bands) * (SIGMA_ONE / HALF_WIDTH)
    for repeat_index in range(filter_degree - 1):
        sigma_next = 1.0 / (2.0 / SIGMA_ONE - sigma_now)
        following = (operate(current, potential) - CENTER * current) * (
            2.0 * sigma_next / HALF_WIDTH
        ) - sigma_now * sigma_next * previous
        previous, current, sigma_now = (current, following, sigma_next)
    applied = operate(current, potential)
    band_count = current.shape[0]
    flat_bands = current.reshape(band_count, -1)
    flat_image = applied.reshape(band_count, -1)
    cell_total = flat_bands.shape[1] * lax.axis_size("grid")
    inverse_cells = 1.0 / cell_total
    first_band = lax.axis_index("band") * band_count
    local_norms = jnp.sum(flat_image * flat_image, axis=1)
    panel_piece = lax.all_gather(current, "band", axis=0, tiled=True)
    flat_piece = panel_piece.reshape(panel_piece.shape[0], -1)
    margin_part = jnp.dot(
        flat_bands,
        flat_piece.T,
        precision=lax.Precision.HIGHEST,
        preferred_element_type=jnp.float32,
    )
    image_part = jnp.dot(
        flat_image,
        flat_piece.T,
        precision=lax.Precision.HIGHEST,
        preferred_element_type=jnp.float32,
    )
    margin_rows = margin_part
    image_rows = image_part
    margin_rows, image_rows, norm_rows = lax.psum((margin_rows, image_rows, local_norms), "grid")
    margin, subspace, image_norms = (
        lax.all_gather(margin_rows, "band", axis=0, tiled=True),
        lax.all_gather(image_rows, "band", axis=0, tiled=True),
        lax.all_gather(norm_rows, "band", axis=0, tiled=True),
    )
    margin = margin * inverse_cells
    subspace = subspace * inverse_cells
    image_norms = image_norms * inverse_cells
    factor = jnp.linalg.cholesky(margin)
    coefficients = lax.linalg.triangular_solve(factor, subspace.T, left_side=True, lower=True)
    projected = lax.linalg.triangular_solve(factor, coefficients.T, left_side=True, lower=True)
    residual_norms = image_norms - jnp.sum(coefficients * coefficients, axis=0)
    projected_rows = lax.dynamic_slice_in_dim(projected, first_band, band_count, 0)
    residual_rows = lax.dynamic_slice_in_dim(residual_norms, first_band, band_count, 0)
    return (current, projected_rows, residual_rows)


def solution(mesh):
    in_specs = (P("band", "grid", None, None), P("grid", None, None))
    out_specs = (P("band", "grid", None, None), P("band", None), P("band"))
    return jax.shard_map(
        on_device, mesh=mesh, in_specs=in_specs, out_specs=out_specs, check_vma=False
    )
```

profile of v0, /device:TPU:32, one launch (start us, length us, event | category | flops | bytes accessed | tf_op | source)
XLA Modules:
  0.0 828.4 jit_solution(4509007590177282399)
XLA Ops:
  7.2 0.9 fusion.157
  8.1 1.9 collective-permute-start
  10.0 16.7 %collective-permute-start.1 = (f32[2,2,32,128]{3,2,1,0:T(8,128)S(1)}, f32[2,2,32,128]{3,2,1,0:T(8,128)S(1)}, u32[]{:S(2)}, u32[]{:S(2)}) collective-permute-start(f32[2,2,32,128]{3,2,1,0:T(8,128)S(1)} %get-tuple-element.100), channel_id=1, source_target_pairs={{1,0},{2,1},{3,2},{4,3},{5,4},{6,5},{7,6},{8,7},{9,8},{10,9},{11,1... | collective-permute-start | bytes 196616 | tf_op jit(solution)/shard_map/ppermute | solution.py:24
  26.8 1.2 fusion.160
  28.0 1.2 fusion.161
  29.2 0.9 fusion.158
  30.2 1.2 fusion.159
  31.4 1.3 fusion.155
  32.6 1.2 fusion.156
  33.9 1.2 fusion.154
  35.0 0.9 broadcast_multiply_fusion.1
  36.0 0.9 fusion.153
  36.9 1.0 constant_dynamic-update-slice_fusion
  38.0 1.7 broadcast_multiply_fusion
  40.0 0.2 fusion.149
  40.4 0.2 fusion.145
  40.6 5.1 collective-permute-start.3
  45.7 1.9 collective-permute-start.2
  47.6 14.4 %collective-permute-done.2 = f32[2,2,32,128]{3,2,1,0:T(8,128)S(1)} collective-permute-done((f32[2,2,32,128]{3,2,1,0:T(8,128)S(1)}, f32[2,2,32,128]{3,2,1,0:T(8,128)S(1)}, u32[]{:S(2)}, u32[]{:S(2)}) %collective-permute-start.2) | collective-permute-done | bytes 65568 | tf_op jit(solution)/shard_map/ppermute | solution.py:22
  62.1 0.7 fusion.65
  62.9 0.2 fusion.139
  63.0 0.2 fusion.140
  63.5 0.2 fusion.136
  63.6 1.9 collective-permute-start.5
  65.5 2.4 collective-permute-start.4
  68.0 14.0 %collective-permute-done.4 = f32[2,2,32,128]{3,2,1,0:T(8,128)S(1)} collective-permute-done((f32[2,2,32,128]{3,2,1,0:T(8,128)S(1)}, f32[2,2,32,128]{3,2,1,0:T(8,128)S(1)}, u32[]{:S(2)}, u32[]{:S(2)}) %collective-permute-start.4) | collective-permute-done | bytes 65568 | tf_op jit(solution)/shard_map/ppermute | solution.py:22
  82.0 0.6 fusion.50
  82.7 0.2 fusion.130
  82.9 0.2 fusion.131
  83.3 0.2 fusion.127
  83.4 1.9 collective-permute-start.7
  85.4 2.4 collective-permute-start.6
  87.8 14.0 %collective-permute-done.6 = f32[2,2,32,128]{3,2,1,0:T(8,128)S(1)} collective-permute-done((f32[2,2,32,128]{3,2,1,0:T(8,128)S(1)}, f32[2,2,32,128]{3,2,1,0:T(8,128)S(1)}, u32[]{:S(2)}, u32[]{:S(2)}) %collective-permute-start.6) | collective-permute-done | bytes 65568 | tf_op jit(solution)/shard_map/ppermute | solution.py:22
  101.8 1.4 fusion.35
  103.2 1.3 dynamic-slice
  105.1 0.9 fusion.121
  106.0 1.9 collective-permute-start.9
  108.0 2.6 collective-permute-start.8
  110.6 0.9 fusion.122
  111.5 1.2 fusion.124
  112.7 1.2 fusion.125
  114.0 1.1 fusion.123
  115.1 1.2 fusion.119
  116.3 1.2 fusion.120
  117.6 1.1 fusion.118
  118.7 0.9 fusion.117
  119.7 4.7 collective-permute-done.8
  124.4 2.4 multiply_reduce_fusion
  126.8 241.7 %all-gather.4.cloned.1.call-done = f32[64,10,32,128]{3,2,1,0:T(8,128)} async-done(((f32[2,10,32,128]{3,2,1,0:T(8,128)}), f32[64,10,32,128]{3,2,1,0:T(8,128)}) %all-gather.4.cloned.1.call-update) | async-done | bytes 10485776 | tf_op jit(solution)/shard_map/all_gather | solution.py:62
  368.4 17.0 %fusion.4 = f32[2,64]{1,0:T(2,128)S(1)} fusion(f32[64,10,32,128]{3,2,1,0:T(8,128)} %all-gather.4.cloned.1.call-done, f32[2,10,32,128]{3,2,1,0:T(8,128)S(1)} %copy-done), kind=kOutput, calls=%fused_computation.4 | convolution fusion | flops 62914560 | bytes 10813952 | tf_op jit(solution)/shard_map/dot_general | solution.py:64
  385.5 12.8 %fusion.7 = f32[2,64]{1,0:T(2,128)S(1)} fusion(f32[64,10,32,128]{3,2,1,0:T(8,128)S(1)} %copy-done.2, f32[2,10,32,128]{3,2,1,0:T(8,128)S(1)} %get-tuple-element.14), kind=kOutput, calls=%fused_computation.5 | convolution fusion | flops 62914560 | bytes 10813952 | tf_op jit(solution)/shard_map/dot_general | solution.py:70
  398.3 62.3 %all-reduce.1 = (f32[2,64]{1,0:T(2,128)S(1)}, f32[2,64]{1,0:T(2,128)S(1)}, f32[2]{0:T(128)S(1)}) all-reduce(f32[2,64]{1,0:T(2,128)S(1)} %fusion.7, f32[2,64]{1,0:T(2,128)S(1)} %fusion.4, f32[2]{0:T(128)S(1)} %get-tuple-element.13), channel_id=1, replica_groups=mesh['band'=32,'grid'=16] {'grid'}, use_global_device_ids=true, to_apply=%region_3.4 | all-reduce | flops 258 | bytes 2064 | tf_op jit(solution)/shard_map/psum | solution.py:78
  460.6 115.9 %all-gather.1 = f32[32,2,64]{2,1,0:T(2,128)S(1)} all-gather(f32[1,2,64]{2,1,0:T(2,128)S(1)} %bitcast.38), channel_id=1, replica_groups=mesh['band'=32,'grid'=16] {'band'}, dimensions={0}, use_global_device_ids=true | all-gather | bytes 16896 | tf_op jit(solution)/shard_map/all_gather | solution.py:81
  576.5 117.9 %all-gather = f32[32,2,64]{2,1,0:T(2,128)S(1)} all-gather(f32[1,2,64]{2,1,0:T(2,128)S(1)} %bitcast.37), channel_id=1, replica_groups=mesh['band'=32,'grid'=16] {'band'}, dimensions={0}, use_global_device_ids=true | all-gather | bytes 16896 | tf_op jit(solution)/shard_map/all_gather | solution.py:80
  694.5 5.8 cholesky.18
  700.4 0.6 compare_reduce_fusion
  701.0 0.7 fusion.108
  701.7 4.9 custom-call.8
  706.6 0.3 multiply_reduce_fusion.1
  706.9 0.2 fusion.109
  707.1 0.2 dynamic-update-slice.3
  707.4 113.1 %all-reduce = f32[64]{0:T(128)S(1)} all-reduce(f32[64]{0:T(128)S(1)} %dynamic-update-slice.3), channel_id=1, replica_groups=mesh['band'=32,'grid'=16] {'band'}, use_global_device_ids=true, to_apply=%add | all-reduce | flops 64 | bytes 512
  820.4 0.6 constant_dynamic-slice_fusion
  821.0 0.6 dynamic_slice.7
  (44 shorter events, 1.4 us)
Async XLA Ops:
  7.2 361.3 %all-gather.4.cloned.1.call-start = ((), (), s32[]{:S(2)}) async-start(), calls=%async_computation | async-start | bytes 10813440 | tf_op jit(solution)/shard_map/all_gather | solution.py:62
  8.1 28.8 %collective-permute-start = (f32[2,2,32,128]{3,2,1,0:T(8,128)S(1)}, f32[2,2,32,128]{3,2,1,0:T(8,128)S(1)}, u32[]{:S(2)}, u32[]{:S(2)}) collective-permute-start(f32[2,2,32,128]{3,2,1,0:T(8,128)S(1)} %get-tuple-element.99), channel_id=1, source_target_pairs={{0,1},{1,2},{2,3},{3,4},{4,5},{5,6},{6,7},{7,8},{8,9},{9,10},{10,1... | collective-permute-start | bytes 196616 | tf_op jit(solution)/shard_map/ppermute | solution.py:22
  10.0 28.0 %collective-permute-start.1 = (f32[2,2,32,128]{3,2,1,0:T(8,128)S(1)}, f32[2,2,32,128]{3,2,1,0:T(8,128)S(1)}, u32[]{:S(2)}, u32[]{:S(2)}) collective-permute-start(f32[2,2,32,128]{3,2,1,0:T(8,128)S(1)} %get-tuple-element.100), channel_id=1, source_target_pairs={{1,0},{2,1},{3,2},{4,3},{5,4},{6,5},{7,6},{8,7},{9,8},{10,9},{11,1... | collective-permute-start | bytes 196616 | tf_op jit(solution)/shard_map/ppermute | solution.py:24
  31.3 30.8 %copy-start.1 = (f32[2,10,32,128]{3,2,1,0:T(8,128)S(1)}, f32[2,10,32,128]{3,2,1,0:T(8,128)}, u32[]{:S(2)}) copy-start(f32[2,10,32,128]{3,2,1,0:T(8,128)} %param.4) | copy-start | bytes 983044
  39.8 42.2 %copy-start.3 = (f32[10,32,128]{2,1,0:T(8,128)S(1)}, f32[10,32,128]{2,1,0:T(8,128)}, u32[]{:S(2)}) copy-start(f32[10,32,128]{2,1,0:T(8,128)} %param.5) | copy-start | bytes 491524
  40.6 7.1 collective-permute-start.3
  45.7 16.4 %collective-permute-start.2 = (f32[2,2,32,128]{3,2,1,0:T(8,128)S(1)}, f32[2,2,32,128]{3,2,1,0:T(8,128)S(1)}, u32[]{:S(2)}, u32[]{:S(2)}) collective-permute-start(f32[2,2,32,128]{3,2,1,0:T(8,128)S(1)} %get-tuple-element.87), channel_id=1, source_target_pairs={{0,1},{1,2},{2,3},{3,4},{4,5},{5,6},{6,7},{7,8},{8,9},{9,10},{10,1... | collective-permute-start | bytes 196616 | tf_op jit(solution)/shard_map/ppermute | solution.py:22
  63.6 4.4 collective-permute-start.5
  65.5 16.4 %collective-permute-start.4 = (f32[2,2,32,128]{3,2,1,0:T(8,128)S(1)}, f32[2,2,32,128]{3,2,1,0:T(8,128)S(1)}, u32[]{:S(2)}, u32[]{:S(2)}) collective-permute-start(f32[2,2,32,128]{3,2,1,0:T(8,128)S(1)} %get-tuple-element.69), channel_id=1, source_target_pairs={{0,1},{1,2},{2,3},{3,4},{4,5},{5,6},{6,7},{7,8},{8,9},{9,10},{10,1... | collective-permute-start | bytes 196616 | tf_op jit(solution)/shard_map/ppermute | solution.py:22
  83.4 4.4 collective-permute-start.7
  85.4 16.4 %collective-permute-start.6 = (f32[2,2,32,128]{3,2,1,0:T(8,128)S(1)}, f32[2,2,32,128]{3,2,1,0:T(8,128)S(1)}, u32[]{:S(2)}, u32[]{:S(2)}) collective-permute-start(f32[2,2,32,128]{3,2,1,0:T(8,128)S(1)} %get-tuple-element.51), channel_id=1, source_target_pairs={{0,1},{1,2},{2,3},{3,4},{4,5},{5,6},{6,7},{7,8},{8,9},{9,10},{10,1... | collective-permute-start | bytes 196616 | tf_op jit(solution)/shard_map/ppermute | solution.py:22
  103.2 265.3 %copy-start = (f32[2,10,32,128]{3,2,1,0:T(8,128)S(1)}, f32[2,10,32,128]{3,2,1,0:T(8,128)}, u32[]{:S(2)}) copy-start(f32[2,10,32,128]{3,2,1,0:T(8,128)} %fusion.35) | copy-start | bytes 983044
  106.0 13.6 %collective-permute-start.9 = (f32[2,2,32,128]{3,2,1,0:T(8,128)S(1)}, f32[2,2,32,128]{3,2,1,0:T(8,128)S(1)}, u32[]{:S(2)}, u32[]{:S(2)}) collective-permute-start(f32[2,2,32,128]{3,2,1,0:T(8,128)S(1)} %get-tuple-element.26), channel_id=1, source_target_pairs={{1,0},{2,1},{3,2},{4,3},{5,4},{6,5},{7,6},{8,7},{9,8},{10,9},{11,1... | collective-permute-start | bytes 196616 | tf_op jit(solution)/shard_map/ppermute | solution.py:24
  108.0 16.4 %collective-permute-start.8 = (f32[2,2,32,128]{3,2,1,0:T(8,128)S(1)}, f32[2,2,32,128]{3,2,1,0:T(8,128)S(1)}, u32[]{:S(2)}, u32[]{:S(2)}) collective-permute-start(f32[2,2,32,128]{3,2,1,0:T(8,128)S(1)} %get-tuple-element.25), channel_id=1, source_target_pairs={{0,1},{1,2},{2,3},{3,4},{4,5},{5,6},{6,7},{7,8},{8,9},{9,10},{10,1... | collective-permute-start | bytes 196616 | tf_op jit(solution)/shard_map/ppermute | solution.py:22
  368.4 17.0 %copy-start.2 = (f32[64,10,32,128]{3,2,1,0:T(8,128)S(1)}, f32[64,10,32,128]{3,2,1,0:T(8,128)}, u32[]{:S(2)}) copy-start(f32[64,10,32,128]{3,2,1,0:T(8,128)} %all-gather.4.cloned.1.call-done) | copy-start | bytes 31457284
Sparse Core Ops, SparseCore 0:
  103.3 265.0 all-gather.3
where the time goes:
time: 829 us; the launch traced here: 828 us
  blocking collectives  409 us (49%)
  waiting for transfers between devices  289 us (35%)
  starting transfers between devices  38.9 us (5%)
  matrix products  30.4 us (4%)
  local copies, waits for them, and re-layouts  26.3 us (3%)
  other arithmetic  19.9 us (2%)
  between operations  15.1 us (2%)
    all_gather x1, waiting for transfers between devices, on_device(): panel_piece = lax.all_gather(current, 'band', axis=0, tiled=True)  242 us
    all_gather x1, blocking collectives, on_device(): lax.all_gather(margin_rows, 'band', axis=0, tiled=True)  118 us
    all_gather x1, blocking collectives, on_device(): lax.all_gather(image_rows, 'band', axis=0, tiled=True)  116 us
    unnamed x1, blocking collectives  113 us
    psum x1, blocking collectives, on_device(): lax.psum((margin_rows, image_rows, local_norms), 'grid')  62.3 us
    ppermute x5, waiting for transfers between devices, padded_2(): lax.ppermute(tail, axis, [(i, (i + 1) % count) for i in range(count)])  47.1 us
    ppermute x5, starting transfers between devices, padded_2(): lax.ppermute(head, axis, [((i + 1) % count, i) for i in range(count)])  27.6 us
    dot_general x1, matrix products, on_device(): jnp.dot(flat_bands, flat_piece.T, precision=lax.Precision.HIGHEST, prefer...  17 us
  transfers between devices with their start and end apart: 11, of which 5 were waited for; matrix products, arithmetic and copies ran while one was open for 3% of the time, Pallas kernels for 0%

commit v1 on v0

--- a/solution.py
+++ b/solution.py
@@ -78,7 +78,9 @@
     margin_rows, image_rows, norm_rows = lax.psum((margin_rows, image_rows, local_norms), "grid")
     margin, subspace, image_norms = (
         lax.all_gather(margin_rows, "band", axis=0, tiled=True),
-        lax.all_gather(image_rows, "band", axis=0, tiled=True),
+        jnp.concatenate(
+            lax.all_to_all(jnp.stack([image_rows] * lax.axis_size("band")), "band", 0, 0), axis=0
+        ),
         lax.all_gather(norm_rows, "band", axis=0, tiled=True),
     )
     margin = margin * inverse_cells

time: 829 us -> 733 us (0.88)
  blocking collectives: 409 us -> 298 us
  starting transfers between devices: 38.9 us -> 51.4 us
    all_gather x1 -> x0, blocking collectives: 116 us -> none  [on_device(): lax.all_gather(image_rows, 'band', axis=0, tiled=True)]
    all_to_all x0 -> x1, starting transfers between devices: none -> 12.6 us  [on_device(): lax.all_to_all(jnp.stack([image_rows] * lax.axis_size('band')), 'band', 0...]
    unnamed x1, blocking collectives: 113 us -> 123 us
  transfers between devices with their start and end apart: 11 -> 12, of which waited for: 5 -> 5; matrix products, arithmetic and copies ran while one was open for 3% -> 5% of each run, Pallas kernels for 0% -> 0%
where the time goes in v1:
time: 733 us; the launch traced here: 731 us
  blocking collectives  298 us (41%)
  waiting for transfers between devices  289 us (39%)
  starting transfers between devices  51.4 us (7%)
  matrix products  30.3 us (4%)
  local copies, waits for them, and re-layouts  27.7 us (4%)
  other arithmetic  20.5 us (3%)
  between operations  15.1 us (2%)
    all_gather x1, waiting for transfers between devices, on_device(): panel_piece = lax.all_gather(current, 'band', axis=0, tiled=True)  242 us
    unnamed x1, blocking collectives  123 us
    all_gather x1, blocking collectives, on_device(): lax.all_gather(margin_rows, 'band', axis=0, tiled=True)  112 us
    psum x1, blocking collectives, on_device(): lax.psum((margin_rows, image_rows, local_norms), 'grid')  62.3 us
    ppermute x5, waiting for transfers between devices, padded_2(): lax.ppermute(tail, axis, [(i, (i + 1) % count) for i in range(count)])  47.1 us
    ppermute x5, starting transfers between devices, padded_2(): lax.ppermute(head, axis, [((i + 1) % count, i) for i in range(count)])  27.6 us
    dot_general x1, matrix products, on_device(): jnp.dot(flat_bands, flat_piece.T, precision=lax.Precision.HIGHEST, prefer...  17 us
  transfers between devices with their start and end apart: 12, of which 5 were waited for; matrix products, arithmetic and copies ran while one was open for 5% of the time, Pallas kernels for 0%

profile of v1, /device:TPU:32, one launch (start us, length us, event | category | flops | bytes accessed | tf_op | source)
XLA Modules:
  0.0 731.5 jit_solution(8606035640182124944)
XLA Ops:
  7.2 0.9 fusion.157
  8.1 1.9 collective-permute-start
  10.0 16.7 %collective-permute-start.1 = (f32[2,2,32,128]{3,2,1,0:T(8,128)S(1)}, f32[2,2,32,128]{3,2,1,0:T(8,128)S(1)}, u32[]{:S(2)}, u32[]{:S(2)}) collective-permute-start(f32[2,2,32,128]{3,2,1,0:T(8,128)S(1)} %get-tuple-element.100), channel_id=1, source_target_pairs={{1,0},{2,1},{3,2},{4,3},{5,4},{6,5},{7,6},{8,7},{9,8},{10,9},{11,1... | collective-permute-start | bytes 196616 | tf_op jit(solution)/shard_map/ppermute | solution.py:24
  26.8 1.2 fusion.160
  28.0 1.2 fusion.161
  29.2 0.9 fusion.158
  30.2 1.2 fusion.159
  31.4 1.3 fusion.155
  32.6 1.2 fusion.156
  33.9 1.2 fusion.154
  35.0 0.9 broadcast_multiply_fusion.1
  36.0 0.9 fusion.153
  36.9 1.0 constant_dynamic-update-slice_fusion
  38.0 1.7 broadcast_multiply_fusion
  40.0 0.2 fusion.149
  40.4 0.2 fusion.145
  40.6 5.1 collective-permute-start.3
  45.7 1.9 collective-permute-start.2
  47.6 14.4 %collective-permute-done.2 = f32[2,2,32,128]{3,2,1,0:T(8,128)S(1)} collective-permute-done((f32[2,2,32,128]{3,2,1,0:T(8,128)S(1)}, f32[2,2,32,128]{3,2,1,0:T(8,128)S(1)}, u32[]{:S(2)}, u32[]{:S(2)}) %collective-permute-start.2) | collective-permute-done | bytes 65568 | tf_op jit(solution)/shard_map/ppermute | solution.py:22
  62.1 0.7 fusion.65
  63.0 0.2 fusion.140
  63.5 0.2 fusion.136
  63.6 1.9 collective-permute-start.5
  65.5 2.4 collective-permute-start.4
  68.0 14.0 %collective-permute-done.4 = f32[2,2,32,128]{3,2,1,0:T(8,128)S(1)} collective-permute-done((f32[2,2,32,128]{3,2,1,0:T(8,128)S(1)}, f32[2,2,32,128]{3,2,1,0:T(8,128)S(1)}, u32[]{:S(2)}, u32[]{:S(2)}) %collective-permute-start.4) | collective-permute-done | bytes 65568 | tf_op jit(solution)/shard_map/ppermute | solution.py:22
  82.0 0.6 fusion.50
  82.9 0.2 fusion.131
  83.4 1.9 collective-permute-start.7
  85.4 2.4 collective-permute-start.6
  87.8 14.0 %collective-permute-done.6 = f32[2,2,32,128]{3,2,1,0:T(8,128)S(1)} collective-permute-done((f32[2,2,32,128]{3,2,1,0:T(8,128)S(1)}, f32[2,2,32,128]{3,2,1,0:T(8,128)S(1)}, u32[]{:S(2)}, u32[]{:S(2)}) %collective-permute-start.6) | collective-permute-done | bytes 65568 | tf_op jit(solution)/shard_map/ppermute | solution.py:22
  101.8 1.4 fusion.35
  103.2 1.3 dynamic-slice
  105.1 0.9 fusion.121
  106.0 1.9 collective-permute-start.9
  108.0 2.6 collective-permute-start.8
  110.6 0.9 fusion.122
  111.5 1.2 fusion.124
  112.7 1.2 fusion.125
  114.0 1.1 fusion.123
  115.1 1.2 fusion.119
  116.3 1.2 fusion.120
  117.6 1.1 fusion.118
  118.7 0.9 fusion.117
  119.7 4.7 collective-permute-done.8
  124.4 2.4 multiply_reduce_fusion
  126.8 241.7 %all-gather.3.cloned.1.call-done = f32[64,10,32,128]{3,2,1,0:T(8,128)} async-done(((f32[2,10,32,128]{3,2,1,0:T(8,128)}), f32[64,10,32,128]{3,2,1,0:T(8,128)}) %all-gather.3.cloned.1.call-update) | async-done | bytes 10485776 | tf_op jit(solution)/shard_map/all_gather | solution.py:62
  368.4 17.0 %fusion.4 = f32[2,64]{1,0:T(2,128)S(1)} fusion(f32[64,10,32,128]{3,2,1,0:T(8,128)} %all-gather.3.cloned.1.call-done, f32[2,10,32,128]{3,2,1,0:T(8,128)S(1)} %copy-done), kind=kOutput, calls=%fused_computation.4 | convolution fusion | flops 62914560 | bytes 10813952 | tf_op jit(solution)/shard_map/dot_general | solution.py:64
  385.5 12.8 %fusion.7 = f32[2,64]{1,0:T(2,128)S(1)} fusion(f32[64,10,32,128]{3,2,1,0:T(8,128)S(1)} %copy-done.2, f32[2,10,32,128]{3,2,1,0:T(8,128)S(1)} %get-tuple-element.14), kind=kOutput, calls=%fused_computation.5 | convolution fusion | flops 62914560 | bytes 10813952 | tf_op jit(solution)/shard_map/dot_general | solution.py:70
  398.3 62.3 %all-reduce.1 = (f32[2,64]{1,0:T(2,128)S(1)}, f32[2,64]{1,0:T(2,128)S(1)}, f32[2]{0:T(128)S(1)}) all-reduce(f32[2,64]{1,0:T(2,128)S(1)} %fusion.7, f32[2,64]{1,0:T(2,128)S(1)} %fusion.4, f32[2]{0:T(128)S(1)} %get-tuple-element.13), channel_id=1, replica_groups=mesh['band'=32,'grid'=16] {'grid'}, use_global_device_ids=true, to_apply=%region_3.4 | all-reduce | flops 258 | bytes 2064 | tf_op jit(solution)/shard_map/psum | solution.py:78
  460.6 0.7 reshape.44
  461.3 12.6 %all-to-all-start = ((f32[32,1,128]{2,1,0:T(1,128)}), f32[32,1,128]{2,1,0:T(1,128)S(1)}, u32[]{:S(2)}, u32[]{:S(2)}) async-start(f32[32,1,128]{2,1,0:T(1,128)} %reshape.44), calls=%async_computation | async-start | bytes 32768 | tf_op jit(solution)/shard_map/all_to_all | solution.py:82
  473.9 112.0 %all-gather = f32[32,2,64]{2,1,0:T(2,128)S(1)} all-gather(f32[1,2,64]{2,1,0:T(2,128)S(1)} %bitcast.36), channel_id=1, replica_groups=mesh['band'=32,'grid'=16] {'band'}, dimensions={0}, use_global_device_ids=true | all-gather | bytes 16896 | tf_op jit(solution)/shard_map/all_gather | solution.py:80
  586.0 5.8 cholesky.18
  591.8 0.6 compare_reduce_fusion
  592.5 0.7 fusion.108
  593.1 4.9 custom-call.8
  598.1 0.2 dynamic-update-slice.3
  598.3 123.3 %all-reduce = f32[64]{0:T(128)S(1)} all-reduce(f32[64]{0:T(128)S(1)} %dynamic-update-slice.3), channel_id=1, replica_groups=mesh['band'=32,'grid'=16] {'band'}, use_global_device_ids=true, to_apply=%add | all-reduce | flops 64 | bytes 512
  721.6 0.5 broadcast.119
  722.1 0.7 reduce.7
  723.0 0.3 multiply_reduce_fusion.1
  723.2 0.2 fusion.109
  723.5 0.6 constant_dynamic-slice_fusion
  724.0 0.6 dynamic_slice.7
  (50 shorter events, 2.0 us)
Async XLA Ops:
  7.2 361.3 %all-gather.3.cloned.1.call-start = ((), (), s32[]{:S(2)}) async-start(), calls=%async_computation.1 | async-start | bytes 10813440 | tf_op jit(solution)/shard_map/all_gather | solution.py:62
  8.1 28.8 %collective-permute-start = (f32[2,2,32,128]{3,2,1,0:T(8,128)S(1)}, f32[2,2,32,128]{3,2,1,0:T(8,128)S(1)}, u32[]{:S(2)}, u32[]{:S(2)}) collective-permute-start(f32[2,2,32,128]{3,2,1,0:T(8,128)S(1)} %get-tuple-element.99), channel_id=1, source_target_pairs={{0,1},{1,2},{2,3},{3,4},{4,5},{5,6},{6,7},{7,8},{8,9},{9,10},{10,1... | collective-permute-start | bytes 196616 | tf_op jit(solution)/shard_map/ppermute | solution.py:22
  10.0 28.0 %collective-permute-start.1 = (f32[2,2,32,128]{3,2,1,0:T(8,128)S(1)}, f32[2,2,32,128]{3,2,1,0:T(8,128)S(1)}, u32[]{:S(2)}, u32[]{:S(2)}) collective-permute-start(f32[2,2,32,128]{3,2,1,0:T(8,128)S(1)} %get-tuple-element.100), channel_id=1, source_target_pairs={{1,0},{2,1},{3,2},{4,3},{5,4},{6,5},{7,6},{8,7},{9,8},{10,9},{11,1... | collective-permute-start | bytes 196616 | tf_op jit(solution)/shard_map/ppermute | solution.py:24
  31.3 30.8 %copy-start.1 = (f32[2,10,32,128]{3,2,1,0:T(8,128)S(1)}, f32[2,10,32,128]{3,2,1,0:T(8,128)}, u32[]{:S(2)}) copy-start(f32[2,10,32,128]{3,2,1,0:T(8,128)} %param.4) | copy-start | bytes 983044
  39.8 42.2 %copy-start.3 = (f32[10,32,128]{2,1,0:T(8,128)S(1)}, f32[10,32,128]{2,1,0:T(8,128)}, u32[]{:S(2)}) copy-start(f32[10,32,128]{2,1,0:T(8,128)} %param.5) | copy-start | bytes 491524
  40.6 7.1 collective-permute-start.3
  45.7 16.4 %collective-permute-start.2 = (f32[2,2,32,128]{3,2,1,0:T(8,128)S(1)}, f32[2,2,32,128]{3,2,1,0:T(8,128)S(1)}, u32[]{:S(2)}, u32[]{:S(2)}) collective-permute-start(f32[2,2,32,128]{3,2,1,0:T(8,128)S(1)} %get-tuple-element.87), channel_id=1, source_target_pairs={{0,1},{1,2},{2,3},{3,4},{4,5},{5,6},{6,7},{7,8},{8,9},{9,10},{10,1... | collective-permute-start | bytes 196616 | tf_op jit(solution)/shard_map/ppermute | solution.py:22
  63.6 4.4 collective-permute-start.5
  65.5 16.4 %collective-permute-start.4 = (f32[2,2,32,128]{3,2,1,0:T(8,128)S(1)}, f32[2,2,32,128]{3,2,1,0:T(8,128)S(1)}, u32[]{:S(2)}, u32[]{:S(2)}) collective-permute-start(f32[2,2,32,128]{3,2,1,0:T(8,128)S(1)} %get-tuple-element.69), channel_id=1, source_target_pairs={{0,1},{1,2},{2,3},{3,4},{4,5},{5,6},{6,7},{7,8},{8,9},{9,10},{10,1... | collective-permute-start | bytes 196616 | tf_op jit(solution)/shard_map/ppermute | solution.py:22
  83.4 4.4 collective-permute-start.7
  85.4 16.4 %collective-permute-start.6 = (f32[2,2,32,128]{3,2,1,0:T(8,128)S(1)}, f32[2,2,32,128]{3,2,1,0:T(8,128)S(1)}, u32[]{:S(2)}, u32[]{:S(2)}) collective-permute-start(f32[2,2,32,128]{3,2,1,0:T(8,128)S(1)} %get-tuple-element.51), channel_id=1, source_target_pairs={{0,1},{1,2},{2,3},{3,4},{4,5},{5,6},{6,7},{7,8},{8,9},{9,10},{10,1... | collective-permute-start | bytes 196616 | tf_op jit(solution)/shard_map/ppermute | solution.py:22
  103.2 265.3 %copy-start = (f32[2,10,32,128]{3,2,1,0:T(8,128)S(1)}, f32[2,10,32,128]{3,2,1,0:T(8,128)}, u32[]{:S(2)}) copy-start(f32[2,10,32,128]{3,2,1,0:T(8,128)} %fusion.35) | copy-start | bytes 983044
  106.0 13.6 %collective-permute-start.9 = (f32[2,2,32,128]{3,2,1,0:T(8,128)S(1)}, f32[2,2,32,128]{3,2,1,0:T(8,128)S(1)}, u32[]{:S(2)}, u32[]{:S(2)}) collective-permute-start(f32[2,2,32,128]{3,2,1,0:T(8,128)S(1)} %get-tuple-element.26), channel_id=1, source_target_pairs={{1,0},{2,1},{3,2},{4,3},{5,4},{6,5},{7,6},{8,7},{9,8},{10,9},{11,1... | collective-permute-start | bytes 196616 | tf_op jit(solution)/shard_map/ppermute | solution.py:24
  108.0 16.4 %collective-permute-start.8 = (f32[2,2,32,128]{3,2,1,0:T(8,128)S(1)}, f32[2,2,32,128]{3,2,1,0:T(8,128)S(1)}, u32[]{:S(2)}, u32[]{:S(2)}) collective-permute-start(f32[2,2,32,128]{3,2,1,0:T(8,128)S(1)} %get-tuple-element.25), channel_id=1, source_target_pairs={{0,1},{1,2},{2,3},{3,4},{4,5},{5,6},{6,7},{7,8},{8,9},{9,10},{10,1... | collective-permute-start | bytes 196616 | tf_op jit(solution)/shard_map/ppermute | solution.py:22
  368.4 17.0 %copy-start.2 = (f32[64,10,32,128]{3,2,1,0:T(8,128)S(1)}, f32[64,10,32,128]{3,2,1,0:T(8,128)}, u32[]{:S(2)}) copy-start(f32[64,10,32,128]{3,2,1,0:T(8,128)} %all-gather.3.cloned.1.call-done) | copy-start | bytes 31457284
  461.3 260.4 %all-to-all-start = ((f32[32,1,128]{2,1,0:T(1,128)}), f32[32,1,128]{2,1,0:T(1,128)S(1)}, u32[]{:S(2)}, u32[]{:S(2)}) async-start(f32[32,1,128]{2,1,0:T(1,128)} %reshape.44), calls=%async_computation | async-start | bytes 32768 | tf_op jit(solution)/shard_map/all_to_all | solution.py:82
Sparse Core Ops, SparseCore 0:
  103.3 265.0 all-gather.2
